TPU v7x, 512 devices: a whole 4x8x8 slice. The times are simulated.
512 devices in a mesh: req: 64 (over x, z, core), ch: 8 (over y).
Axes of the slice: x: 4, y: 8, z: 8, core: 2. Of those that a mesh axis runs over, the one named last changes fastest.
Arguments:
- tokens: bfloat16 [128, 4096], P('req', 'ch'), may hold values from -80 to 80
- attn_gain: float32 [4096], P('ch'), may hold values from 0.1 to 1.9
- w_query: bfloat16 [4096, 4096], P('ch', 'req'), may hold values from -0.09375 to 0.09375
- w_keyval: bfloat16 [4096, 512], P('ch', 'req'), may hold values from -0.09375 to 0.09375
- cache: bfloat16 [2, 128, 256, 2048], P(None, 'req', 'ch'), may hold values from -70 to 70
- lengths: int32 [128], P('req'), may hold values from 1 to 2047, as said below
- write_pos: int32 [128], P('req'), may hold values from 0 to 2047
- w_out: bfloat16 [4096, 4096], P('ch', 'req'), may hold values from -0.09375 to 0.09375
- mlp_gain: float32 [4096], P('ch'), may hold values from 0.1 to 1.9
- w_gate_up: bfloat16 [4096, 24576], P('ch', 'req'), may hold values from -0.09375 to 0.09375
- w_down: bfloat16 [12288, 4096], P('req', 'ch'), may hold values from -0.0546875 to 0.0546875
Outputs:
- layer_out: bfloat16 [128, 4096], P('req', 'ch')
- kv_new: bfloat16 [128, 512], P('req', 'ch')
Inputs may be any that keep to these rules, and one draw needn't show every extreme that they name: lengths[b] earlier tokens of request b are in the cache; the largest equals 2047 in every draw. The new token of request b goes to slot write_pos[b]; its earlier tokens fill the slots before it, going back cyclically.
All inputs are finite; a program needn't handle non-finite values.
Results may differ from a plain program's by a relative error of at most 0.0064.
Values may be sent and summed in bfloat16 or wider, within the bound.
No kernel may reach another device: no remote copies, remote signals or barrier semaphores. Data moves between devices by JAX's collectives and lax.ppermute only.
A program may use at most 64 MiB of HBM per device.

v0:
```python
import math
import jax
import jax.numpy as jnp
from jax import lax
from jax.sharding import PartitionSpec as P

D = 4096
H = 16
HD = 256
EPSILON = 1e-06


def rms_norm(values, gain):
    wide = values.astype(jnp.float32)
    squares = jnp.sum(wide * wide, axis=1)
    summed = lax.psum(squares, "ch")
    meansq = summed / D
    return (wide * lax.rsqrt(meansq + EPSILON)[:, None] * gain[None, :]).astype(jnp.bfloat16)


def body(
    tokens,
    attn_gain,
    w_query,
    w_keyval,
    cache,
    lengths,
    write_pos,
    w_out,
    mlp_gain,
    w_gate_up,
    w_down,
):
    rows = tokens.shape[0]
    chan = cache.shape[2]
    window = cache.shape[3]
    factor = 1.0 / math.sqrt(HD)
    normed = rms_norm(tokens, attn_gain)
    joined = jnp.concatenate([w_query, w_keyval], axis=1)
    head_parts = jnp.dot(
        lax.all_gather(normed, "req", axis=0, tiled=True),
        joined,
        preferred_element_type=jnp.float32,
    )
    query_cols = w_query.shape[1]
    query_part, keyval_part = (
        lax.all_to_all(head_parts[:, :query_cols], "req", split_axis=0, concat_axis=1, tiled=True),
        lax.all_to_all(head_parts[:, query_cols:], "req", split_axis=0, concat_axis=1, tiled=True),
    )
    query_sum, keyval_sum = (
        lax.psum_scatter(query_part, "ch", scatter_dimension=1, tiled=True),
        lax.psum_scatter(keyval_part, "ch", scatter_dimension=1, tiled=True),
    )
    queries = query_sum.astype(jnp.bfloat16).reshape(rows, H, chan)
    keyval_new = keyval_sum.astype(jnp.bfloat16)
    key_new = keyval_new[:, :chan]
    value_new = keyval_new[:, chan:]
    keys = cache[0]
    values_cache = cache[1]
    own_part = jnp.sum(
        queries.astype(jnp.float32) * key_new.astype(jnp.float32)[:, None, :], axis=-1
    )
    score_part = jnp.einsum("bhe,bew->bhw", queries, keys, preferred_element_type=jnp.float32)
    summed, own_sum = lax.psum((score_part, own_part), "ch")
    slot_index = jnp.arange(window, dtype=jnp.int32)
    offset = (write_pos[:, None] - 1 - slot_index[None, :]) % window
    usable = offset < lengths[:, None]
    scores = jnp.where(usable[:, None, :], summed * factor, -jnp.inf)
    own_score = own_sum * factor
    top = jnp.maximum(jnp.max(scores, axis=-1), own_score)
    weights = jnp.exp(scores - top[..., None])
    own_weight = jnp.exp(own_score - top)
    total = jnp.sum(weights, axis=-1) + own_weight
    weights_low = weights.astype(jnp.bfloat16)
    numer = jnp.einsum(
        "bhw,bew->bhe", weights_low, values_cache, preferred_element_type=jnp.float32
    )
    numer = (
        numer
        + own_weight.astype(jnp.bfloat16).astype(jnp.float32)[..., None]
        * value_new.astype(jnp.float32)[:, None, :]
    )
    attn_local = (numer / total[..., None]).astype(jnp.bfloat16).reshape(rows, H * chan)
    out_parts = jnp.dot(
        lax.all_gather(attn_local, "req", axis=0, tiled=True),
        w_out,
        preferred_element_type=jnp.float32,
    )
    out_part = lax.all_to_all(out_parts, "req", split_axis=0, concat_axis=1, tiled=True)
    out_sum = lax.psum_scatter(out_part, "ch", scatter_dimension=1, tiled=True)
    first = (tokens.astype(jnp.float32) + out_sum).astype(jnp.bfloat16)
    normed_two = rms_norm(first, mlp_gain)
    hidden_cols = w_gate_up.shape[1] // 2
    ffn_parts = jnp.dot(
        lax.all_gather(normed_two, "req", axis=0, tiled=True),
        w_gate_up,
        preferred_element_type=jnp.float32,
    )
    ffn_total = lax.psum(ffn_parts, "ch")
    hidden = (
        jax.nn.gelu(ffn_total[:, :hidden_cols], approximate=True) * ffn_total[:, hidden_cols:]
    ).astype(jnp.bfloat16)
    down_sum = lax.psum_scatter(
        jnp.dot(hidden, w_down, preferred_element_type=jnp.float32),
        "req",
        scatter_dimension=0,
        tiled=True,
    )
    layer_out = (first.astype(jnp.float32) + down_sum).astype(jnp.bfloat16)
    return (layer_out, keyval_new)


def solution(mesh):
    placed = (
        P("req", "ch"),
        P("ch"),
        P("ch", "req"),
        P("ch", "req"),
        P(None, "req", "ch", None),
        P("req"),
        P("req"),
        P("ch", "req"),
        P("ch"),
        P("ch", "req"),
        P("req", "ch"),
    )
    return jax.shard_map(
        body,
        mesh=mesh,
        in_specs=placed,
        out_specs=(P("req", "ch"), P("req", "ch")),
        check_vma=False,
    )
```

profile of v0, /device:TPU:1, one launch (start us, length us, event | category | flops | bytes accessed | tf_op | source)
XLA Modules:
  0.0 728.1 jit_solution(11447148937282177522)
XLA Ops:
  7.2 0.8 fusion.36
  8.0 14.7 %psum.35 = f32[2]{0:T(128)S(1)} all-reduce(f32[2]{0:T(128)S(1)} %fusion.36), channel_id=1, replica_groups=mesh['req'=64,'ch'=8] {'ch'}, use_global_device_ids=true, to_apply=%region_1.0 | all-reduce | flops 2 | bytes 16 | tf_op jit(solution)/shard_map/psum | solution.py:16
  23.5 60.2 %all-gather = bf16[64,2,512]{2,1,0:T(2,128)(2,1)S(1)} all-gather(bf16[1,2,512]{2,1,0:T(2,128)(2,1)S(1)} %fusion.45), channel_id=1, replica_groups=mesh['req'=64,'ch'=8] {'req'}, dimensions={0}, use_global_device_ids=true | all-gather | bytes 133120 | tf_op jit(solution)/shard_map/all_gather | solution.py:41
  83.7 1.0 fusion.24
  85.5 5.6 all-to-all-start.1
  91.9 8.9 %all-to-all-done.1 = f32[64,2,8]{2,1,0:T(2,128)S(1)} async-done(((f32[64,2,8]{2,1,0:T(2,128)}), f32[64,2,8]{2,1,0:T(2,128)S(1)}, u32[]{:S(2)}, u32[]{:S(2)}) %all-to-all-start.1) | async-done | bytes 4128 | tf_op jit(solution)/shard_map/all_to_all | solution.py:48
  100.8 4.4 all-to-all-start
  105.2 1.2 copy.40
  107.2 7.5 %all-to-all-done = f32[64,1,128]{2,1,0:T(1,128)S(1)} async-done(((f32[64,1,128]{2,1,0:T(1,128)}), f32[64,1,128]{2,1,0:T(1,128)S(1)}, u32[]{:S(2)}, u32[]{:S(2)}) %all-to-all-start) | async-done | bytes 32800 | tf_op jit(solution)/shard_map/all_to_all | solution.py:47
  116.0 2.0 copy.39
  118.2 23.1 %reduce-scatter.12.cloned.1.call-done = f32[64,2]{1,0:T(8,128)} async-done(((f32[512,2]{1,0:T(8,128)}), f32[64,2]{1,0:T(8,128)}) %reduce-scatter.12.cloned.1.call-update) | async-done | bytes 528
  142.2 47.1 %reduce-scatter.10.cloned.1.call-done = f32[512,2]{1,0:T(8,128)} async-done(((f32[4096,2]{1,0:T(8,128)}), f32[512,2]{1,0:T(8,128)}) %reduce-scatter.10.cloned.1.call-update) | async-done | bytes 4112
  189.3 1.1 copy.34
  190.5 0.9 fusion.3
  191.6 11.9 %psum.37 = f32[2,16]{1,0:T(2,128)S(1)} all-reduce(f32[2,16]{1,0:T(2,128)S(1)} %multiply_reduce_fusion), channel_id=1, replica_groups=mesh['req'=64,'ch'=8] {'ch'}, use_global_device_ids=true, to_apply=%region_7.8 | all-reduce | flops 32 | bytes 256 | tf_op jit(solution)/shard_map/psum | solution.py:64
  203.5 64.4 %all-reduce.5.cloned.1.call-done = f32[2,16,2048]{2,1,0:T(8,128)} async-done(((f32[2,16,2048]{2,1,0:T(8,128)}), f32[2,16,2048]{2,1,0:T(8,128)}) %all-reduce.5.cloned.1.call-update) | async-done | bytes 262160 | tf_op jit(solution)/shard_map/psum | solution.py:64
  267.9 1.1 fusion.7
  269.0 1.2 fusion.8
  270.1 1.2 fusion.1
  271.4 57.0 %all-gather.1 = bf16[64,2,512]{2,1,0:T(2,128)(2,1)S(1)} all-gather(bf16[1,2,512]{2,1,0:T(2,128)(2,1)S(1)} %reshape.73), channel_id=1, replica_groups=mesh['req'=64,'ch'=8] {'req'}, dimensions={0}, use_global_device_ids=true | all-gather | bytes 133120 | tf_op jit(solution)/shard_map/all_gather | solution.py:85
  328.8 16.1 %all_to_all.57 = f32[64,1,128]{2,1,0:T(1,128)S(1)} all-to-all(f32[64,1,128]{2,1,0:T(1,128)S(1)} %reshape.87), channel_id=1, replica_groups=mesh['req'=64,'ch'=8] {'req'}, dimensions={0} | all-to-all | bytes 65536 | tf_op jit(solution)/shard_map/all_to_all | solution.py:89
  345.8 2.0 copy.41
  347.9 32.4 %reduce-scatter.14.cloned.1.call-done = f32[512,2]{1,0:T(8,128)} async-done(((f32[4096,2]{1,0:T(8,128)}), f32[512,2]{1,0:T(8,128)}) %reduce-scatter.14.cloned.1.call-update) | async-done | bytes 4112
  380.3 1.1 copy.38
  381.5 12.0 %psum.38 = f32[2]{0:T(128)S(1)} all-reduce(f32[2]{0:T(128)S(1)} %get-tuple-element.2), channel_id=1, replica_groups=mesh['req'=64,'ch'=8] {'ch'}, use_global_device_ids=true, to_apply=%region_11.12 | all-reduce | flops 2 | bytes 16 | tf_op jit(solution)/shard_map/psum | solution.py:16
  393.6 59.6 %all-gather.2 = bf16[64,2,512]{2,1,0:T(2,128)(2,1)S(1)} all-gather(bf16[1,2,512]{2,1,0:T(2,128)(2,1)S(1)} %fusion.44), channel_id=1, replica_groups=mesh['req'=64,'ch'=8] {'req'}, dimensions={0}, use_global_device_ids=true | all-gather | bytes 133120 | tf_op jit(solution)/shard_map/all_gather | solution.py:95
  453.2 0.9 fusion.56
  454.2 69.2 %all-reduce.7.cloned.1.call-done = f32[128,384]{1,0:T(8,128)} async-done(((f32[128,384]{1,0:T(8,128)}), f32[128,384]{1,0:T(8,128)}) %all-reduce.7.cloned.1.call-update) | async-done | bytes 196624 | tf_op jit(solution)/shard_map/psum | solution.py:99
  523.4 1.9 fusion.28
  525.3 1.3 dynamic-slice
  527.3 192.7 %all-reduce.9.cloned.1.call-done = f32[128,512]{1,0:T(8,128)} async-done(((f32[128,512]{1,0:T(8,128)}), f32[128,512]{1,0:T(8,128)}) %all-reduce.9.cloned.1.call-update) | async-done | bytes 262160
  720.0 1.3 fusion.43
  (57 shorter events, 7.5 us)
Async XLA Ops:
  7.2 446.1 %copy-start = (bf16[512,384]{1,0:T(8,128)(2,1)S(1)}, bf16[512,384]{1,0:T(8,128)(2,1)}, u32[]{:S(2)}) copy-start(bf16[512,384]{1,0:T(8,128)(2,1)} %param.20) | copy-start | bytes 1179652
  85.5 15.3 %all-to-all-start.1 = ((f32[64,2,8]{2,1,0:T(2,128)}), f32[64,2,8]{2,1,0:T(2,128)S(1)}, u32[]{:S(2)}, u32[]{:S(2)}) async-start(f32[64,2,8]{2,1,0:T(2,128)} %bitcast.4), calls=%async_computation.1 | async-start | bytes 131072 | tf_op jit(solution)/shard_map/all_to_all | solution.py:48
  100.8 13.8 %all-to-all-start = ((f32[64,1,128]{2,1,0:T(1,128)}), f32[64,1,128]{2,1,0:T(1,128)S(1)}, u32[]{:S(2)}, u32[]{:S(2)}) async-start(f32[64,1,128]{2,1,0:T(1,128)} %reshape.85), calls=%async_computation | async-start | bytes 65536 | tf_op jit(solution)/shard_map/all_to_all | solution.py:47
  105.2 36.1 %reduce-scatter.12.cloned.1.call-start = ((), (), s32[]{:S(2)}) async-start(), calls=%async_computation.9 | async-start | bytes 294912
  106.4 82.9 %reduce-scatter.10.cloned.1.call-start = ((), (), s32[]{:S(2)}) async-start(), calls=%async_computation.8 | async-start | bytes 2359296
  116.0 2.2 copy-start.7
  116.0 74.5 %copy-start.2 = (bf16[2,2,32,2048]{3,2,1,0:T(8,128)(2,1)S(1)}, bf16[2,2,32,2048]{3,2,1,0:T(8,128)(2,1)}, u32[]{:S(2)}) copy-start(bf16[2,2,32,2048]{3,2,1,0:T(8,128)(2,1)} %param.15) | copy-start | bytes 1572868
  118.0 210.5 %copy-start.3 = (bf16[512,64]{0,1:T(8,128)(2,1)S(1)}, bf16[512,64]{0,1:T(8,128)(2,1)}, u32[]{:S(2)}) copy-start(bf16[512,64]{0,1:T(8,128)(2,1)} %param.18) | copy-start | bytes 196612
  118.1 149.8 %all-reduce.5.cloned.1.call-start = ((), (), s32[]{:S(2)}) async-start(), calls=%async_computation.6 | async-start | bytes 524288 | tf_op jit(solution)/shard_map/psum | solution.py:64
  142.2 205.6 %copy-start.5 = (bf16[2,64]{1,0:T(2,128)(2,1)}, bf16[2,64]{1,0:T(2,128)(2,1)S(1)}, u32[]{:S(2)}) copy-start(bf16[2,64]{1,0:T(2,128)(2,1)S(1)} %copy.36) | copy-start | bytes 772
  191.4 188.9 %reduce-scatter.14.cloned.1.call-start = ((), (), s32[]{:S(2)}) async-start(), calls=%async_computation.10 | async-start | bytes 2359296
  345.7 35.6 %copy-start.4 = (bf16[2,512]{1,0:T(2,128)(2,1)S(1)}, bf16[2,512]{1,0:T(2,128)(2,1)}, u32[]{:S(2)}) copy-start(bf16[2,512]{1,0:T(2,128)(2,1)} %param.11) | copy-start | bytes 6148
  345.8 47.8 %copy-start.6 = (f32[512]{0:T(512)S(1)}, f32[512]{0:T(512)}, u32[]{:S(2)}) copy-start(f32[512]{0:T(512)} %param.19) | copy-start | bytes 6148
  347.8 175.6 %copy-start.1 = (bf16[192,512]{1,0:T(8,128)(2,1)S(1)}, bf16[192,512]{1,0:T(8,128)(2,1)}, u32[]{:S(2)}) copy-start(bf16[192,512]{1,0:T(8,128)(2,1)} %param.21) | copy-start | bytes 589828
  347.8 175.6 %all-reduce.7.cloned.1.call-start = ((), (), s32[]{:S(2)}) async-start(), calls=%async_computation.7 | async-start | bytes 393216 | tf_op jit(solution)/shard_map/psum | solution.py:99
  454.2 265.8 %all-reduce.9.cloned.1.call-start = ((), (), s32[]{:S(2)}) async-start(), calls=%async_computation.11 | async-start | bytes 524288
Sparse Core Ops, SparseCore 0:
  108.8 32.4 reduce-scatter.11
  144.2 45.0 reduce-scatter.9
  191.6 76.2 all-reduce.4
  348.0 32.2 reduce-scatter.13
  454.3 69.0 all-reduce.6
  526.7 193.2 all-reduce.8
where the time goes:
time: 729 us; the launch traced here: 728 us
  waiting for transfers between devices  446 us (61%)
  blocking collectives  231 us (32%)
  between operations  15 us (2%)
  local copies, waits for them, and re-layouts  12.2 us (2%)
  starting transfers between devices  10.2 us (1%)
  other arithmetic  7.74 us (1%)
    unnamed x10, waiting for transfers between devices  295 us
    psum x1, waiting for transfers between devices, body(): ffn_total = lax.psum(ffn_parts, 'ch')  69.2 us
    psum x1, waiting for transfers between devices, body(): summed, own_sum = lax.psum((score_part, own_part), 'ch')  64.4 us
    all_gather x1, blocking collectives, body(): lax.all_gather(normed, 'req', axis=0, tiled=True)  60.2 us
    all_gather x1, blocking collectives, body(): lax.all_gather(normed_two, 'req', axis=0, tiled=True)  59.6 us
    all_gather x1, blocking collectives, body(): lax.all_gather(attn_local, 'req', axis=0, tiled=True)  57 us
    psum x2, blocking collectives, rms_norm(): summed = lax.psum(squares, 'ch')  26.7 us
    all_to_all x1, blocking collectives, body(): lax.all_to_all(out_parts, 'req', split_axis=0, concat_axis=1, tiled=True)  16.1 us
  transfers between devices with their start and end apart: 8, of which 8 were waited for; matrix products, arithmetic and copies ran while one was open for 1% of the time, Pallas kernels for 0%

commit v1 on v0

--- a/solution.py
+++ b/solution.py
@@ -96,7 +96,11 @@
         w_gate_up,
         preferred_element_type=jnp.float32,
     )
-    ffn_total = lax.psum(ffn_parts, "ch")
+    ffn_total = ffn_parts
+    for hop in (1, 2, 4):
+        ffn_total = ffn_total + lax.ppermute(
+            ffn_total, "ch", [(dev, dev ^ hop) for dev in range(8)]
+        )
     hidden = (
         jax.nn.gelu(ffn_total[:, :hidden_cols], approximate=True) * ffn_total[:, hidden_cols:]
     ).astype(jnp.bfloat16)

time: 729 us -> 686 us (0.941)
  waiting for transfers between devices: 446 us -> 392 us
  starting transfers between devices: 10.2 us -> 22 us
    psum x1 -> x0, waiting for transfers between devices: 69.2 us -> none  [body(): ffn_total = lax.psum(ffn_parts, 'ch')]
    ppermute x0 -> x3, waiting for transfers between devices: none -> 24.7 us  [body(): lax.ppermute(ffn_total, 'ch', [(dev, dev ^ hop) for dev in range(8)])]
    ppermute x0 -> x3, starting transfers between devices: none -> 11.9 us  [body(): lax.ppermute(ffn_total, 'ch', [(dev, dev ^ hop) for dev in range(8)])]
    unnamed x10 -> x9, waiting for transfers between devices: 295 us -> 287 us
  transfers between devices with their start and end apart: 8 -> 10, of which waited for: 8 -> 10; matrix products, arithmetic and copies ran while one was open for 1% -> 1% of each run, Pallas kernels for 0% -> 0%
where the time goes in v1:
time: 686 us; the launch traced here: 685 us
  waiting for transfers between devices  392 us (57%)
  blocking collectives  231 us (34%)
  starting transfers between devices  22 us (3%)
  between operations  14.7 us (2%)
  local copies, waits for them, and re-layouts  12.2 us (2%)
  other arithmetic  7.81 us (1%)
    unnamed x9, waiting for transfers between devices  287 us
    psum x1, waiting for transfers between devices, body(): summed, own_sum = lax.psum((score_part, own_part), 'ch')  64.4 us
    all_gather x1, blocking collectives, body(): lax.all_gather(normed, 'req', axis=0, tiled=True)  60.2 us
    all_gather x1, blocking collectives, body(): lax.all_gather(normed_two, 'req', axis=0, tiled=True)  59.6 us
    all_gather x1, blocking collectives, body(): lax.all_gather(attn_local, 'req', axis=0, tiled=True)  57 us
    psum x2, blocking collectives, rms_norm(): summed = lax.psum(squares, 'ch')  26.7 us
    ppermute x3, waiting for transfers between devices, body(): lax.ppermute(ffn_total, 'ch', [(dev, dev ^ hop) for dev in range(8)])  24.7 us
    all_to_all x1, blocking collectives, body(): lax.all_to_all(out_parts, 'req', split_axis=0, concat_axis=1, tiled=True)  16.1 us
  transfers between devices with their start and end apart: 10, of which 10 were waited for; matrix products, arithmetic and copies ran while one was open for 1% of the time, Pallas kernels for 0%

profile of v1, /device:TPU:1, one launch (start us, length us, event | category | flops | bytes accessed | tf_op | source)
XLA Modules:
  0.0 685.1 jit_solution(15757812545150767217)
XLA Ops:
  8.0 14.7 %psum.28 = f32[2]{0:T(128)S(1)} all-reduce(f32[2]{0:T(128)S(1)} %fusion.36), channel_id=1, replica_groups=mesh['req'=64,'ch'=8] {'ch'}, use_global_device_ids=true, to_apply=%region_1.0 | all-reduce | flops 2 | bytes 16 | tf_op jit(solution)/shard_map/psum | solution.py:16
  23.5 60.2 %all-gather = bf16[64,2,512]{2,1,0:T(2,128)(2,1)S(1)} all-gather(bf16[1,2,512]{2,1,0:T(2,128)(2,1)S(1)} %fusion.45), channel_id=1, replica_groups=mesh['req'=64,'ch'=8] {'req'}, dimensions={0}, use_global_device_ids=true | all-gather | bytes 133120 | tf_op jit(solution)/shard_map/all_gather | solution.py:41
  85.5 5.6 all-to-all-start.1
  91.9 8.9 %all-to-all-done.1 = f32[64,2,8]{2,1,0:T(2,128)S(1)} async-done(((f32[64,2,8]{2,1,0:T(2,128)}), f32[64,2,8]{2,1,0:T(2,128)S(1)}, u32[]{:S(2)}, u32[]{:S(2)}) %all-to-all-start.1) | async-done | bytes 4128 | tf_op jit(solution)/shard_map/all_to_all | solution.py:48
  100.8 4.4 all-to-all-start
  105.2 1.2 copy.40
  107.2 7.5 %all-to-all-done = f32[64,1,128]{2,1,0:T(1,128)S(1)} async-done(((f32[64,1,128]{2,1,0:T(1,128)}), f32[64,1,128]{2,1,0:T(1,128)S(1)}, u32[]{:S(2)}, u32[]{:S(2)}) %all-to-all-start) | async-done | bytes 32800 | tf_op jit(solution)/shard_map/all_to_all | solution.py:47
  116.0 2.0 copy.39
  118.2 23.1 %reduce-scatter.12.cloned.1.call-done = f32[64,2]{1,0:T(8,128)} async-done(((f32[512,2]{1,0:T(8,128)}), f32[64,2]{1,0:T(8,128)}) %reduce-scatter.12.cloned.1.call-update) | async-done | bytes 528
  142.2 47.1 %reduce-scatter.10.cloned.1.call-done = f32[512,2]{1,0:T(8,128)} async-done(((f32[4096,2]{1,0:T(8,128)}), f32[512,2]{1,0:T(8,128)}) %reduce-scatter.10.cloned.1.call-update) | async-done | bytes 4112
  189.3 1.1 copy.34
  191.6 11.9 %psum.30 = f32[2,16]{1,0:T(2,128)S(1)} all-reduce(f32[2,16]{1,0:T(2,128)S(1)} %multiply_reduce_fusion), channel_id=1, replica_groups=mesh['req'=64,'ch'=8] {'ch'}, use_global_device_ids=true, to_apply=%region_7.8 | all-reduce | flops 32 | bytes 256 | tf_op jit(solution)/shard_map/psum | solution.py:64
  203.5 64.4 %all-reduce.4.cloned.1.call-done = f32[2,16,2048]{2,1,0:T(8,128)} async-done(((f32[2,16,2048]{2,1,0:T(8,128)}), f32[2,16,2048]{2,1,0:T(8,128)}) %all-reduce.4.cloned.1.call-update) | async-done | bytes 262160 | tf_op jit(solution)/shard_map/psum | solution.py:64
  267.9 1.1 fusion.7
  269.0 1.2 fusion.8
  270.1 1.2 fusion.1
  271.4 57.0 %all-gather.1 = bf16[64,2,512]{2,1,0:T(2,128)(2,1)S(1)} all-gather(bf16[1,2,512]{2,1,0:T(2,128)(2,1)S(1)} %reshape.73), channel_id=1, replica_groups=mesh['req'=64,'ch'=8] {'req'}, dimensions={0}, use_global_device_ids=true | all-gather | bytes 133120 | tf_op jit(solution)/shard_map/all_gather | solution.py:85
  328.8 16.1 %all_to_all.57 = f32[64,1,128]{2,1,0:T(1,128)S(1)} all-to-all(f32[64,1,128]{2,1,0:T(1,128)S(1)} %reshape.87), channel_id=1, replica_groups=mesh['req'=64,'ch'=8] {'req'}, dimensions={0} | all-to-all | bytes 65536 | tf_op jit(solution)/shard_map/all_to_all | solution.py:89
  345.8 2.0 copy.41
  347.9 32.4 %reduce-scatter.14.cloned.1.call-done = f32[512,2]{1,0:T(8,128)} async-done(((f32[4096,2]{1,0:T(8,128)}), f32[512,2]{1,0:T(8,128)}) %reduce-scatter.14.cloned.1.call-update) | async-done | bytes 4112
  380.3 1.1 copy.38
  381.5 12.0 %psum.31 = f32[2]{0:T(128)S(1)} all-reduce(f32[2]{0:T(128)S(1)} %get-tuple-element.2), channel_id=1, replica_groups=mesh['req'=64,'ch'=8] {'ch'}, use_global_device_ids=true, to_apply=%region_11.12 | all-reduce | flops 2 | bytes 16 | tf_op jit(solution)/shard_map/psum | solution.py:16
  393.6 59.6 %all-gather.2 = bf16[64,2,512]{2,1,0:T(2,128)(2,1)S(1)} all-gather(bf16[1,2,512]{2,1,0:T(2,128)(2,1)S(1)} %fusion.44), channel_id=1, replica_groups=mesh['req'=64,'ch'=8] {'req'}, dimensions={0}, use_global_device_ids=true | all-gather | bytes 133120 | tf_op jit(solution)/shard_map/all_gather | solution.py:95
  453.5 2.5 collective-permute-start
  456.0 5.7 collective-permute-done
  461.7 2.9 collective-permute-start.1
  464.6 10.6 %collective-permute-done.1 = f32[128,384]{1,0:T(8,128)S(1)} collective-permute-done((f32[128,384]{1,0:T(8,128)S(1)}, f32[128,384]{1,0:T(8,128)S(1)}, u32[]{:S(2)}, u32[]{:S(2)}) %collective-permute-start.1) | collective-permute-done | bytes 196640 | tf_op jit(solution)/shard_map/ppermute | solution.py:101
  475.2 6.5 collective-permute-start.2
  481.8 8.4 %collective-permute-done.2 = f32[128,384]{1,0:T(8,128)S(1)} collective-permute-done((f32[128,384]{1,0:T(8,128)S(1)}, f32[128,384]{1,0:T(8,128)S(1)}, u32[]{:S(2)}, u32[]{:S(2)}) %collective-permute-start.2) | collective-permute-done | bytes 196640 | tf_op jit(solution)/shard_map/ppermute | solution.py:101
  491.2 1.3 dynamic-slice
  493.1 184.2 %all-reduce.6.cloned.1.call-done = f32[128,512]{1,0:T(8,128)} async-done(((f32[128,512]{1,0:T(8,128)}), f32[128,512]{1,0:T(8,128)}) %all-reduce.6.cloned.1.call-update) | async-done | bytes 262160
  677.3 1.3 fusion.43
  (63 shorter events, 11.4 us)
Async XLA Ops:
  7.2 446.1 %copy-start = (bf16[512,384]{1,0:T(8,128)(2,1)S(1)}, bf16[512,384]{1,0:T(8,128)(2,1)}, u32[]{:S(2)}) copy-start(bf16[512,384]{1,0:T(8,128)(2,1)} %param.20) | copy-start | bytes 1179652
  85.5 15.3 %all-to-all-start.1 = ((f32[64,2,8]{2,1,0:T(2,128)}), f32[64,2,8]{2,1,0:T(2,128)S(1)}, u32[]{:S(2)}, u32[]{:S(2)}) async-start(f32[64,2,8]{2,1,0:T(2,128)} %bitcast.4), calls=%async_computation.1 | async-start | bytes 131072 | tf_op jit(solution)/shard_map/all_to_all | solution.py:48
  100.8 13.8 %all-to-all-start = ((f32[64,1,128]{2,1,0:T(1,128)}), f32[64,1,128]{2,1,0:T(1,128)S(1)}, u32[]{:S(2)}, u32[]{:S(2)}) async-start(f32[64,1,128]{2,1,0:T(1,128)} %reshape.85), calls=%async_computation | async-start | bytes 65536 | tf_op jit(solution)/shard_map/all_to_all | solution.py:47
  105.2 36.1 %reduce-scatter.12.cloned.1.call-start = ((), (), s32[]{:S(2)}) async-start(), calls=%async_computation.8 | async-start | bytes 294912
  106.4 82.9 %reduce-scatter.10.cloned.1.call-start = ((), (), s32[]{:S(2)}) async-start(), calls=%async_computation.7 | async-start | bytes 2359296
  116.0 2.2 copy-start.7
  116.0 74.5 %copy-start.2 = (bf16[2,2,32,2048]{3,2,1,0:T(8,128)(2,1)S(1)}, bf16[2,2,32,2048]{3,2,1,0:T(8,128)(2,1)}, u32[]{:S(2)}) copy-start(bf16[2,2,32,2048]{3,2,1,0:T(8,128)(2,1)} %param.15) | copy-start | bytes 1572868
  118.0 210.5 %copy-start.3 = (bf16[512,64]{0,1:T(8,128)(2,1)S(1)}, bf16[512,64]{0,1:T(8,128)(2,1)}, u32[]{:S(2)}) copy-start(bf16[512,64]{0,1:T(8,128)(2,1)} %param.18) | copy-start | bytes 196612
  118.1 149.8 %all-reduce.4.cloned.1.call-start = ((), (), s32[]{:S(2)}) async-start(), calls=%async_computation.6 | async-start | bytes 524288 | tf_op jit(solution)/shard_map/psum | solution.py:64
  142.2 205.6 %copy-start.5 = (bf16[2,64]{1,0:T(2,128)(2,1)}, bf16[2,64]{1,0:T(2,128)(2,1)S(1)}, u32[]{:S(2)}) copy-start(bf16[2,64]{1,0:T(2,128)(2,1)S(1)} %copy.36) | copy-start | bytes 772
  191.4 188.9 %reduce-scatter.14.cloned.1.call-start = ((), (), s32[]{:S(2)}) async-start(), calls=%async_computation.9 | async-start | bytes 2359296
  345.7 35.6 %copy-start.4 = (bf16[2,512]{1,0:T(2,128)(2,1)S(1)}, bf16[2,512]{1,0:T(2,128)(2,1)}, u32[]{:S(2)}) copy-start(bf16[2,512]{1,0:T(2,128)(2,1)} %param.11) | copy-start | bytes 6148
  345.8 47.8 %copy-start.6 = (f32[512]{0:T(512)S(1)}, f32[512]{0:T(512)}, u32[]{:S(2)}) copy-start(f32[512]{0:T(512)} %param.19) | copy-start | bytes 6148
  347.8 142.4 %copy-start.1 = (bf16[192,512]{1,0:T(8,128)(2,1)S(1)}, bf16[192,512]{1,0:T(8,128)(2,1)}, u32[]{:S(2)}) copy-start(bf16[192,512]{1,0:T(8,128)(2,1)} %param.21) | copy-start | bytes 589828
  347.9 329.4 %all-reduce.6.cloned.1.call-start = ((), (), s32[]{:S(2)}) async-start(), calls=%async_computation.10 | async-start | bytes 524288
  453.5 8.2 %collective-permute-start = (f32[128,384]{1,0:T(8,128)S(1)}, f32[128,384]{1,0:T(8,128)S(1)}, u32[]{:S(2)}, u32[]{:S(2)}) collective-permute-start(f32[128,384]{1,0:T(8,128)S(1)} %fusion.56), channel_id=1, source_target_pairs={{0,1},{1,0},{2,3},{3,2},{4,5},{5,4},{6,7},{7,6},{8,9},{9,8},{10,11... | collective-permute-start | bytes 589832 | tf_op jit(solution)/shard_map/ppermute | solution.py:101
  461.7 13.5 %collective-permute-start.1 = (f32[128,384]{1,0:T(8,128)S(1)}, f32[128,384]{1,0:T(8,128)S(1)}, u32[]{:S(2)}, u32[]{:S(2)}) collective-permute-start(f32[128,384]{1,0:T(8,128)S(1)} %add.70), channel_id=1, source_target_pairs={{0,2},{1,3},{2,0},{3,1},{4,6},{5,7},{6,4},{7,5},{8,10},{9,11},{10,... | collective-permute-start | bytes 589832 | tf_op jit(solution)/shard_map/ppermute | solution.py:101
  475.2 15.0 %collective-permute-start.2 = (f32[128,384]{1,0:T(8,128)S(1)}, f32[128,384]{1,0:T(8,128)S(1)}, u32[]{:S(2)}, u32[]{:S(2)}) collective-permute-start(f32[128,384]{1,0:T(8,128)S(1)} %add.71), channel_id=1, source_target_pairs={{0,4},{1,5},{2,6},{3,7},{4,0},{5,1},{6,2},{7,3},{8,12},{9,13},{10,... | collective-permute-start | bytes 589832 | tf_op jit(solution)/shard_map/ppermute | solution.py:101
Sparse Core Ops, SparseCore 0:
  108.8 32.4 reduce-scatter.11
  144.2 45.0 reduce-scatter.9
  191.6 76.2 all-reduce.3
  348.0 32.2 reduce-scatter.13
  491.3 185.9 all-reduce.5
